TPU v7x, 256 devices: a whole 4x4x8 slice. The times are simulated.
256 devices in a mesh: shots: 8 (over z_hi, y), slab: 32 (over z_lo, x, core).
Axes of the slice: x: 4, y: 4, z: 8 (z_hi: 2, z_lo: 4; z = z_hi * 4 + z_lo), core: 2. Of those that a mesh axis runs over, the one named last changes fastest.
Arguments:
- vel_parts: float32 [8, 128, 512, 256], P('shots', 'slab'), may hold values from -24 to 24
- den_parts: float32 [8, 128, 512, 256], P('shots', 'slab'), may hold values from -24 to 24
- illum_parts: float32 [8, 128, 512, 256], P('shots', 'slab'), may hold values from 0.02 to 0.2
- layer_index: int32 [256], replicated, may hold values from 0 to 15, never falling along the last dimension, each value on 1 to 128 neighbouring positions
- depth_scale: float32 [2, 16], replicated, may hold values from 1 to 8
Outputs:
- vel_update: float32 [128, 512, 256], P('slab')
- den_update: float32 [128, 512, 256], P('slab')
Inputs may be any that keep to these rules, and one draw needn't show every extreme that they name: `layer_index`: never falls with depth; every layer holds 1 to 128 consecutive depth cells, and one holds exactly 128.
All inputs are finite; a program needn't handle non-finite values.
Results may differ from a plain program's by a relative error of at most 0.00011.
Values sent between devices are 32-bit elements; how exact they have to be, the bound alone decides.
No kernel may reach another device: no remote copies, remote signals or barrier semaphores. Data moves between devices by JAX's collectives and lax.ppermute only.
A program may use at most 64 MiB of HBM per device.

v0:
```python
import jax
import jax.numpy as jnp
from jax import lax
from jax.sharding import PartitionSpec as P

RADIUS = 20


def smoothing_matrix(count):
    cells = jnp.arange(count, dtype=jnp.int32)
    offset = (cells[:, None] - cells[None, :]).astype(jnp.float32)
    inside = jnp.abs(offset) <= RADIUS
    weights = jnp.where(inside, jnp.exp(-offset * offset / 200.0), jnp.float32(0.0))
    return weights / jnp.sum(weights, axis=1, keepdims=True)


def smooth_depth(field):
    matrix = smoothing_matrix(field.shape[2])
    return jnp.einsum("xyj,ij->xyi", field, matrix, precision=lax.Precision.HIGHEST)


def smooth_across(field):
    matrix = smoothing_matrix(field.shape[1])
    return jnp.einsum("ij,xjz->xiz", matrix, field, precision=lax.Precision.HIGHEST)


def smooth_along_x(pieces):
    matrix = smoothing_matrix(pieces[0].shape[0])
    vel_cols = jnp.einsum("ij,jyz->iyz", matrix, pieces[0], precision=lax.Precision.HIGHEST)
    den_cols = jnp.einsum("ij,jyz->iyz", matrix, pieces[1], precision=lax.Precision.HIGHEST)
    return (
        lax.all_to_all(vel_cols, "slab", split_axis=0, concat_axis=1, tiled=True),
        lax.all_to_all(den_cols, "slab", split_axis=0, concat_axis=1, tiled=True),
    )


def cross_slabs(vel, den):
    return smooth_along_x(
        (
            lax.all_to_all(vel, "slab", split_axis=1, concat_axis=0, tiled=True),
            lax.all_to_all(den, "slab", split_axis=1, concat_axis=0, tiled=True),
        )
    )


def body(vel_parts, den_parts, illum_parts, layer_index, depth_scale):
    vel_mine = vel_parts[0]
    den_mine = den_parts[0]
    illum_mine = illum_parts[0]
    vel, den, illum = lax.psum((vel_mine, den_mine, illum_mine), "shots")
    vel, den = cross_slabs(vel / illum, den / illum)
    vel = smooth_depth(smooth_across(vel))
    den = smooth_depth(smooth_across(den))
    onehot = (
        layer_index[:, None] == jnp.arange(depth_scale.shape[1], dtype=jnp.int32)[None, :]
    ).astype(jnp.float32)
    per_depth = jnp.dot(depth_scale, onehot.T, precision=lax.Precision.HIGHEST)
    vel_update = per_depth[0][None, None, :] * vel
    den_update = per_depth[1][None, None, :] * den
    return (vel_update, den_update)


def solution(mesh):
    placed = (
        P("shots", "slab", None, None),
        P("shots", "slab", None, None),
        P("shots", "slab", None, None),
        P(),
        P(),
    )
    return jax.shard_map(
        body,
        mesh=mesh,
        in_specs=placed,
        out_specs=(P("slab", None, None), P("slab", None, None)),
        check_vma=False,
    )
```

profile of v0, /device:TPU:2, one launch (start us, length us, event | category | flops | bytes accessed | tf_op | source)
XLA Modules:
  0.0 561.9 jit_solution(1820788667867668634)
XLA Ops:
  7.2 0.0 copy-start
  7.2 0.0 copy-start.3
  7.2 0.0 all-reduce.3.cloned.1.call-start
  7.2 0.0 copy-start.4
  7.2 4.4 copy.48
  11.7 0.0 copy-done.3
  11.7 0.0 copy-done.4
  11.7 4.7 copy_bitcast_fusion.1
  16.4 0.0 all-reduce.3.cloned.1.call-update
  16.4 278.4 %all-reduce.3.cloned.1.call-done = (f32[4,512,256]{2,0,1:T(4,128)}, f32[4,512,256]{2,0,1:T(4,128)}, f32[4,512,256]{2,0,1:T(4,128)}) async-done(((f32[4,512,256]{2,0,1:T(4,128)}, f32[4,512,256]{2,0,1:T(4,128)}, f32[4,512,256]{2,0,1:T(4,128)}), (f32[4,512,256]{2,0,1:T(4,128)}, f32[4,512,256]{2,0,1:T(4,128)}, f32[4,512,256]{2,0,1:T(4,128)})) %all-reduce.3.cloned.1.call-update) | async-done | bytes 6291472 | tf_op jit(solution)/shard_map/psum | solution.py:50
  294.9 4.6 fusion.60
  299.5 53.3 %all_to_all.72 = f32[4,512,256]{2,0,1:T(4,128)} all-to-all(f32[4,512,256]{2,0,1:T(4,128)S(1)} %bitcast.67), channel_id=1, replica_groups=mesh['shots'=8,'slab'=32] {'slab'}, dimensions={1} | all-to-all | bytes 4194304 | tf_op jit(solution)/shard_map/all_to_all | solution.py:40
  352.8 5.8 %all-to-all-start.2 = ((f32[4,512,256]{2,0,1:T(4,128)}), f32[4,512,256]{2,0,1:T(4,128)S(1)}, u32[]{:S(2)}, u32[]{:S(2)}) async-start(f32[4,512,256]{2,0,1:T(4,128)} %bitcast.64), calls=%async_computation.2 | async-start | bytes 4194304 | tf_op jit(solution)/shard_map/all_to_all | solution.py:41
  358.6 0.1 fusion.38
  358.7 3.5 copy.47
  362.2 3.0 all_to_all.55
  365.2 3.5 fusion.35
  368.7 2.5 copy.27
  371.2 35.8 %all-to-all-done.2 = f32[4,512,256]{2,0,1:T(4,128)S(1)} async-done(((f32[4,512,256]{2,0,1:T(4,128)}), f32[4,512,256]{2,0,1:T(4,128)S(1)}, u32[]{:S(2)}, u32[]{:S(2)}) %all-to-all-start.2) | async-done | bytes 2097184 | tf_op jit(solution)/shard_map/all_to_all | solution.py:41
  407.0 0.0 copy-start.1
  407.0 1.3 copy-done.1
  408.3 17.6 %all-to-all-start.1 = ((f32[128,16,256]{2,1,0:T(8,128)}), f32[128,16,256]{2,1,0:T(8,128)S(1)}, u32[]{:S(2)}, u32[]{:S(2)}) async-start(f32[128,16,256]{2,1,0:T(8,128)} %copy.27), calls=%async_computation.1 | async-start | bytes 4194304 | tf_op jit(solution)/shard_map/all_to_all | solution.py:32
  426.0 3.5 copy.46
  429.5 2.9 all_to_all.63
  432.4 3.5 fusion.33
  435.9 2.5 copy.33
  438.4 0.0 copy-start.5
  438.4 35.9 %all-to-all-done.1 = f32[128,16,256]{2,1,0:T(8,128)S(1)} async-done(((f32[128,16,256]{2,1,0:T(8,128)}), f32[128,16,256]{2,1,0:T(8,128)S(1)}, u32[]{:S(2)}, u32[]{:S(2)}) %all-to-all-start.1) | async-done | bytes 2097184 | tf_op jit(solution)/shard_map/all_to_all | solution.py:32
  474.3 6.1 %all-to-all-start.3 = ((f32[128,16,256]{2,1,0:T(8,128)}), f32[128,16,256]{2,1,0:T(8,128)}, u32[]{:S(2)}, u32[]{:S(2)}) async-start(f32[128,16,256]{2,1,0:T(8,128)} %copy.33), calls=%async_computation.3 | async-start | bytes 4194304 | tf_op jit(solution)/shard_map/all_to_all | solution.py:33
  480.4 0.2 fusion.27
  480.6 0.5 fusion.18
  481.1 0.0 copy-done
  481.1 0.0 copy-done.5
  481.1 0.2 convolution_bitcast_fusion
  481.3 1.6 copy.28
  482.9 46.0 %all-to-all-done.3 = f32[128,16,256]{2,1,0:T(8,128)} async-done(((f32[128,16,256]{2,1,0:T(8,128)}), f32[128,16,256]{2,1,0:T(8,128)}, u32[]{:S(2)}, u32[]{:S(2)}) %all-to-all-start.3) | async-done | bytes 2097184 | tf_op jit(solution)/shard_map/all_to_all | solution.py:33
  528.9 0.0 copy-start.2
  528.9 1.9 copy.34
  530.8 0.3 copy-done.2
  531.1 6.9 %fusion.15 = f32[4,256,512]{2,1,0:T(8,128)S(1)} fusion(f32[4,512,256]{2,1,0:T(8,128)S(1)} %bitcast.76, f32[512]{0:T(512)S(1)} %fusion.18), kind=kOutput, calls=%fused_computation.18 | convolution fusion | flops 3223584768 | bytes 4196352 | tf_op jit(solution)/shard_map/ij,xjz->xiz/dot_general | solution.py:24
  538.0 7.1 %fusion.13 = f32[4,256,512]{2,1,0:T(8,128)S(1)} fusion(f32[4,512,256]{2,1,0:T(8,128)S(1)} %bitcast.77, f32[512]{0:T(512)S(1)} %fusion.18), kind=kOutput, calls=%fused_computation.16 | convolution fusion | flops 3223584768 | bytes 4196352 | tf_op jit(solution)/shard_map/ij,xjz->xiz/dot_general | solution.py:24
  545.0 4.8 fusion.4
  549.9 4.8 fusion.7
  (1 shorter events, 0.0 us)
Async XLA Ops:
  7.2 473.9 %copy-start = (f32[2,16]{1,0:T(2,128)S(1)}, f32[2,16]{1,0:T(2,128)}, u32[]{:S(2)}) copy-start(f32[2,16]{1,0:T(2,128)} %param.9) | copy-start | bytes 388
  7.2 4.5 copy-start.3
  7.2 287.7 %all-reduce.3.cloned.1.call-start = ((), (), s32[]{:S(2)}) async-start(), calls=%async_computation.4 | async-start | bytes 12582912 | tf_op jit(solution)/shard_map/psum | solution.py:50
  7.2 4.4 copy-start.4
  352.8 54.2 %all-to-all-start.2 = ((f32[4,512,256]{2,0,1:T(4,128)}), f32[4,512,256]{2,0,1:T(4,128)S(1)}, u32[]{:S(2)}, u32[]{:S(2)}) async-start(f32[4,512,256]{2,0,1:T(4,128)} %bitcast.64), calls=%async_computation.2 | async-start | bytes 4194304 | tf_op jit(solution)/shard_map/all_to_all | solution.py:41
  407.0 1.3 copy-start.1
  408.3 66.0 %all-to-all-start.1 = ((f32[128,16,256]{2,1,0:T(8,128)}), f32[128,16,256]{2,1,0:T(8,128)S(1)}, u32[]{:S(2)}, u32[]{:S(2)}) async-start(f32[128,16,256]{2,1,0:T(8,128)} %copy.27), calls=%async_computation.1 | async-start | bytes 4194304 | tf_op jit(solution)/shard_map/all_to_all | solution.py:32
  438.4 42.7 %copy-start.5 = (s32[256]{0:T(256)S(1)}, s32[256]{0:T(256)}, u32[]{:S(2)}) copy-start(s32[256]{0:T(256)} %param.8) | copy-start | bytes 3076
  474.3 54.6 %all-to-all-start.3 = ((f32[128,16,256]{2,1,0:T(8,128)}), f32[128,16,256]{2,1,0:T(8,128)}, u32[]{:S(2)}, u32[]{:S(2)}) async-start(f32[128,16,256]{2,1,0:T(8,128)} %copy.33), calls=%async_computation.3 | async-start | bytes 4194304 | tf_op jit(solution)/shard_map/all_to_all | solution.py:33
  528.9 2.2 copy-start.2
Sparse Core Ops, SparseCore 0:
  16.5 278.2 all-reduce.2
where the time goes:
time: 571 us; the launch traced here: 562 us
  waiting for transfers between devices  396 us (69%)
  blocking collectives  53.3 us (9%)
  local copies, waits for them, and re-layouts  32.2 us (6%)
  matrix products  30.8 us (5%)
  starting transfers between devices  29.6 us (5%)
  between operations  14.5 us (3%)
    psum x1, waiting for transfers between devices, body(): vel, den, illum = lax.psum((vel_mine, den_mine, illum_mine), 'shots')  278 us
    all_to_all x1, blocking collectives, cross_slabs(): lax.all_to_all(vel, 'slab', split_axis=1, concat_axis=0, tiled=True)  53.3 us
    all_to_all x1, waiting for transfers between devices, smooth_along_x(): lax.all_to_all(den_cols, 'slab', split_axis=0, concat_axis=1, tiled=True)  46 us
    all_to_all x1, waiting for transfers between devices, smooth_along_x(): lax.all_to_all(vel_cols, 'slab', split_axis=0, concat_axis=1, tiled=True)  35.9 us
    all_to_all x1, waiting for transfers between devices, cross_slabs(): lax.all_to_all(den, 'slab', split_axis=1, concat_axis=0, tiled=True)  35.8 us
    all_to_all x1, starting transfers between devices, smooth_along_x(): lax.all_to_all(vel_cols, 'slab', split_axis=0, concat_axis=1, tiled=True)  17.6 us
    dot_general x2, matrix products, smooth_across(): jnp.einsum('ij,xjz->xiz', matrix, field, precision=lax.Precision.HIGHEST)  13.9 us
  transfers between devices with their start and end apart: 4, of which 4 were waited for; matrix products, arithmetic and copies ran while one was open for 4% of the time, Pallas kernels for 0%

commit v1 on v0

v1 whole, which is shorter than its diff:
```python
import jax
import jax.numpy as jnp
from jax import lax
from jax.sharding import PartitionSpec as P

RADIUS = 20
HP = lax.Precision.HIGHEST


def smoothing_matrix(count):
    cells = jnp.arange(count, dtype=jnp.int32)
    offset = (cells[:, None] - cells[None, :]).astype(jnp.float32)
    inside = jnp.abs(offset) <= RADIUS
    weights = jnp.where(inside, jnp.exp(-offset * offset / 200.0), jnp.float32(0.0))
    return weights / jnp.sum(weights, axis=1, keepdims=True)


def smooth_depth(field):
    matrix = smoothing_matrix(field.shape[2])
    return jnp.einsum("xyj,ij->xyi", field, matrix, precision=HP)


def smooth_across(field):
    matrix = smoothing_matrix(field.shape[1])
    return jnp.einsum("ij,xjz->xiz", matrix, field, precision=HP)


def smooth_along_x(field):
    cols = lax.all_to_all(field, "slab", split_axis=1, concat_axis=0, tiled=True)
    matrix = smoothing_matrix(cols.shape[0])
    cols = jnp.einsum("ij,jyz->iyz", matrix, cols, precision=HP)
    return lax.all_to_all(cols, "slab", split_axis=0, concat_axis=1, tiled=True)


def body(vel_parts, den_parts, illum_parts, layer_index, depth_scale):
    vel, den, illum = lax.psum_scatter(
        (vel_parts[0], den_parts[0], illum_parts[0]), "shots", scatter_dimension=1, tiled=True
    )
    vel = smooth_along_x(smooth_depth(vel / illum))
    den = smooth_along_x(smooth_depth(den / illum))
    vel, den = lax.all_gather((vel, den), "shots", axis=1, tiled=True)
    vel = smooth_across(vel)
    den = smooth_across(den)
    onehot = (
        layer_index[:, None] == jnp.arange(depth_scale.shape[1], dtype=jnp.int32)[None, :]
    ).astype(jnp.float32)
    per_depth = jnp.dot(depth_scale, onehot.T, precision=HP)
    vel_update = per_depth[0][None, None, :] * vel
    den_update = per_depth[1][None, None, :] * den
    return (vel_update, den_update)


def solution(mesh):
    placed = (
        P("shots", "slab", None, None),
        P("shots", "slab", None, None),
        P("shots", "slab", None, None),
        P(),
        P(),
    )
    return jax.shard_map(
        body,
        mesh=mesh,
        in_specs=placed,
        out_specs=(P("slab", None, None), P("slab", None, None)),
        check_vma=False,
    )
```

time: 571 us -> 471 us (0.82); the launches traced: 562 us -> 470 us
  waiting for transfers between devices: 396 us -> 370 us
  local copies, waits for them, and re-layouts: 32.2 us -> 7.19 us
  starting transfers between devices: 29.6 us -> 5.25 us
  matrix products: 30.8 us -> 21.3 us
    psum x1 -> x0, waiting for transfers between devices: 278 us -> none  [body(): vel, den, illum = lax.psum((vel_mine, den_mine, illum_mine), 'shots')]
    reduce_scatter x0 -> x3, waiting for transfers between devices: none -> 251 us  [body(): lax.psum_scatter((vel_parts[0], den_parts[0], illum_parts[0]), 'shots', s...]
    all_to_all x3 -> x1, waiting for transfers between devices: 118 us -> 13 us  [smooth_along_x(): lax.all_to_all(field, 'slab', split_axis=1, concat_axis=0, tiled=True)]
    all_gather x0 -> x2, waiting for transfers between devices: none -> 104 us  [body(): vel, den = lax.all_gather((vel, den), 'shots', axis=1, tiled=True)]
    all_to_all x3 -> x1, starting transfers between devices: 29.6 us -> 5.05 us  [smooth_along_x(): lax.all_to_all(field, 'slab', split_axis=1, concat_axis=0, tiled=True)]
    all_to_all x6 -> x8, local copies, waits for them, and re-layouts: 16.4 us -> 2.08 us  [the longest x4 1.86 us: smooth_along_x(): return lax.all_to_all(cols, 'slab', split_axis=0, concat_axis=1, tiled=True)]
    dot_general x7, matrix products: 30.8 us -> 21.3 us  [the longest x2 17.3 us: smooth_across(): return jnp.einsum('ij,xjz->xiz', matrix, field, precision=HP)]
    all_to_all x1 -> x3, blocking collectives: 53.3 us -> 51.9 us  [the longest x2 37.6 us: smooth_along_x(): return lax.all_to_all(cols, 'slab', split_axis=0, concat_axis=1, tiled=True)]
  transfers between devices with their start and end apart: 4 -> 6, of which waited for: 4 -> 6; matrix products, arithmetic and copies ran while one was open for 4% -> 4% of each run, Pallas kernels for 0% -> 0%
where the time goes in v1:
time: 471 us; the launch traced here: 470 us
  waiting for transfers between devices  370 us (79%)
  blocking collectives  51.9 us (11%)
  matrix products  21.3 us (5%)
  between operations  13.9 us (3%)
  local copies, waits for them, and re-layouts  7.19 us (2%)
  starting transfers between devices  5.25 us (1%)
    reduce_scatter x3, waiting for transfers between devices, body(): lax.psum_scatter((vel_parts[0], den_parts[0], illum_parts[0]), 'shots', s...  251 us
    all_gather x2, waiting for transfers between devices, body(): vel, den = lax.all_gather((vel, den), 'shots', axis=1, tiled=True)  104 us
    all_to_all x2, blocking collectives, smooth_along_x(): return lax.all_to_all(cols, 'slab', split_axis=0, concat_axis=1, tiled=True)  37.6 us
    dot_general x2, matrix products, smooth_across(): return jnp.einsum('ij,xjz->xiz', matrix, field, precision=HP)  17.3 us
    all_to_all x1, blocking collectives, smooth_along_x(): lax.all_to_all(field, 'slab', split_axis=1, concat_axis=0, tiled=True)  14.3 us
    all_to_all x1, waiting for transfers between devices, smooth_along_x(): lax.all_to_all(field, 'slab', split_axis=1, concat_axis=0, tiled=True)  13 us
  transfers between devices with their start and end apart: 6, of which 6 were waited for; matrix products, arithmetic and copies ran while one was open for 4% of the time, Pallas kernels for 0%

profile of v1, /device:TPU:2, one launch (start us, length us, event | category | flops | bytes accessed | tf_op | source)
XLA Modules:
  0.0 470.3 jit_solution(18192071430133639715)
XLA Ops:
  7.2 0.0 copy-start
  7.2 0.0 reduce-scatter.8.cloned.1.call-start
  7.2 0.7 reduce-scatter.8.cloned.1.call-update
  7.9 0.0 reduce-scatter.6.cloned.1.call-start
  8.0 0.7 reduce-scatter.6.cloned.1.call-update
  8.7 0.0 reduce-scatter.4.cloned.1.call-start
  8.7 0.7 reduce-scatter.4.cloned.1.call-update
  9.4 0.2 fusion.18
  9.6 100.9 %reduce-scatter.8.cloned.1.call-done = f32[4,64,256]{2,1,0:T(8,128)} async-done(((f32[4,512,256]{2,1,0:T(8,128)}), f32[4,64,256]{2,1,0:T(8,128)}) %reduce-scatter.8.cloned.1.call-update) | async-done | bytes 262160 | tf_op jit(solution)/shard_map/reduce_scatter | solution.py:36
  110.5 95.7 %reduce-scatter.6.cloned.1.call-done = f32[4,64,256]{2,1,0:T(8,128)} async-done(((f32[4,512,256]{2,1,0:T(8,128)}), f32[4,64,256]{2,1,0:T(8,128)}) %reduce-scatter.6.cloned.1.call-update) | async-done | bytes 262160 | tf_op jit(solution)/shard_map/reduce_scatter | solution.py:36
  206.1 1.5 fusion.12
  207.7 0.9 copy.17
  208.5 5.0 %all-to-all-start.2 = ((f32[4,64,256]{2,0,1:T(4,128)}), f32[4,64,256]{2,0,1:T(4,128)S(1)}, u32[]{:S(2)}, u32[]{:S(2)}) async-start(f32[4,64,256]{2,0,1:T(4,128)} %copy.17), calls=%async_computation.5 | async-start | bytes 524288 | tf_op jit(solution)/shard_map/all_to_all | solution.py:29
  213.6 0.0 copy-start.1
  213.6 0.0 all-gather.5.cloned.1.call-start
  213.7 0.1 fusion.30
  213.8 13.0 %all-to-all-done.2 = f32[4,64,256]{2,0,1:T(4,128)S(1)} async-done(((f32[4,64,256]{2,0,1:T(4,128)}), f32[4,64,256]{2,0,1:T(4,128)S(1)}, u32[]{:S(2)}, u32[]{:S(2)}) %all-to-all-start.2) | async-done | bytes 262176 | tf_op jit(solution)/shard_map/all_to_all | solution.py:29
  226.8 0.1 all_to_all.63
  226.9 0.4 fusion.25
  227.4 0.2 copy.19
  227.6 19.7 %all_to_all.72 = f32[128,2,256]{2,1,0:T(2,128)S(1)} all-to-all(f32[128,2,256]{2,1,0:T(2,128)S(1)} %copy.19), channel_id=1, replica_groups=mesh['shots'=8,'slab'=32] {'slab'}, dimensions={0} | all-to-all | bytes 524288 | tf_op jit(solution)/shard_map/all_to_all | solution.py:32
  247.3 0.9 all_to_all.67
  248.2 0.0 all-gather.5.cloned.1.call-update
  248.2 0.0 all-gather.3.cloned.1.call-start
  248.3 54.5 %reduce-scatter.4.cloned.1.call-done = f32[4,64,256]{2,1,0:T(8,128)} async-done(((f32[4,512,256]{2,1,0:T(8,128)}), f32[4,64,256]{2,1,0:T(8,128)}) %reduce-scatter.4.cloned.1.call-update) | async-done | bytes 262160 | tf_op jit(solution)/shard_map/reduce_scatter | solution.py:36
  302.7 0.0 copy-done.1
  302.7 1.5 fusion.14
  304.2 0.2 copy.13
  304.4 14.3 %all_to_all.73 = f32[4,64,256]{2,0,1:T(4,128)S(1)} all-to-all(f32[4,64,256]{2,0,1:T(4,128)S(1)} %copy.13), channel_id=1, replica_groups=mesh['shots'=8,'slab'=32] {'slab'}, dimensions={1} | all-to-all | bytes 524288 | tf_op jit(solution)/shard_map/all_to_all | solution.py:29
  318.7 0.0 copy-start.2
  318.7 0.1 all_to_all.55
  318.8 0.4 fusion.27
  319.3 0.2 copy.15
  319.5 17.9 %all_to_all.74 = f32[128,2,256]{2,1,0:T(2,128)S(1)} all-to-all(f32[128,2,256]{2,1,0:T(2,128)S(1)} %copy.15), channel_id=1, replica_groups=mesh['shots'=8,'slab'=32] {'slab'}, dimensions={0} | all-to-all | bytes 524288 | tf_op jit(solution)/shard_map/all_to_all | solution.py:32
  337.5 0.9 all_to_all.59
  338.3 0.0 all-gather.3.cloned.1.call-update
  338.4 0.5 fusion.6
  338.8 0.0 copy-done
  338.8 0.0 copy-done.2
  338.8 0.2 convolution_bitcast_fusion
  339.0 39.1 %all-gather.5.cloned.1.call-done = f32[4,512,256]{2,1,0:T(8,128)} async-done(((f32[4,64,256]{2,1,0:T(8,128)}), f32[4,512,256]{2,1,0:T(8,128)}) %all-gather.5.cloned.1.call-update) | async-done | bytes 2097168 | tf_op jit(solution)/shard_map/all_gather | solution.py:41
  378.1 8.6 %multiply_bitcast_fusion = f32[4,512,256]{1,2,0:T(8,128)S(1)} fusion(f32[4,512,256]{2,1,0:T(8,128)} %all-gather.5.cloned.1.call-done, f32[256]{0:T(256)S(1)} %bitcast.63, f32[512]{0:T(512)S(1)} %fusion.6), kind=kOutput, calls=%fused_computation | convolution fusion | flops 3224109056 | bytes 4197376 | tf_op jit(solution)/shard_map/ij,xjz->xiz/dot_general | solution.py:25
  386.8 1.8 copy.22
  388.6 64.7 %all-gather.3.cloned.1.call-done = f32[4,512,256]{2,1,0:T(8,128)} async-done(((f32[4,64,256]{2,1,0:T(8,128)}), f32[4,512,256]{2,1,0:T(8,128)}) %all-gather.3.cloned.1.call-update) | async-done | bytes 2097168 | tf_op jit(solution)/shard_map/all_gather | solution.py:41
  453.3 8.7 %multiply_bitcast_fusion.1 = f32[4,512,256]{1,2,0:T(8,128)S(1)} fusion(f32[4,512,256]{2,1,0:T(8,128)} %all-gather.3.cloned.1.call-done, f32[256]{0:T(256)S(1)} %bitcast.62, f32[512]{0:T(512)S(1)} %fusion.6), kind=kOutput, calls=%fused_computation.1 | convolution fusion | flops 3224109056 | bytes 4197376 | tf_op jit(solution)/shard_map/ij,xjz->xiz/dot_general | solution.py:25
  461.9 1.8 copy.21
  (5 shorter events, 0.1 us)
Async XLA Ops:
  7.2 331.7 %copy-start = (f32[2,16]{1,0:T(2,128)S(1)}, f32[2,16]{1,0:T(2,128)}, u32[]{:S(2)}) copy-start(f32[2,16]{1,0:T(2,128)} %param.9) | copy-start | bytes 388
  7.2 103.3 %reduce-scatter.8.cloned.1.call-start = ((), (), s32[]{:S(2)}) async-start(), calls=%async_computation.10 | async-start | bytes 2359296 | tf_op jit(solution)/shard_map/reduce_scatter | solution.py:36
  7.9 198.2 %reduce-scatter.6.cloned.1.call-start = ((), (), s32[]{:S(2)}) async-start(), calls=%async_computation.8 | async-start | bytes 2359296 | tf_op jit(solution)/shard_map/reduce_scatter | solution.py:36
  8.7 294.0 %reduce-scatter.4.cloned.1.call-start = ((), (), s32[]{:S(2)}) async-start(), calls=%async_computation.7 | async-start | bytes 2359296 | tf_op jit(solution)/shard_map/reduce_scatter | solution.py:36
  208.5 18.3 %all-to-all-start.2 = ((f32[4,64,256]{2,0,1:T(4,128)}), f32[4,64,256]{2,0,1:T(4,128)S(1)}, u32[]{:S(2)}, u32[]{:S(2)}) async-start(f32[4,64,256]{2,0,1:T(4,128)} %copy.17), calls=%async_computation.5 | async-start | bytes 524288 | tf_op jit(solution)/shard_map/all_to_all | solution.py:29
  213.6 89.1 %copy-start.1 = (f32[4,64,256]{2,1,0:T(8,128)S(1)}, f32[4,64,256]{2,1,0:T(8,128)}, u32[]{:S(2)}) copy-start(f32[4,64,256]{2,1,0:T(8,128)} %reduce-scatter.6.cloned.1.call-done) | copy-start | bytes 786436
  213.6 164.5 %all-gather.5.cloned.1.call-start = ((), (), s32[]{:S(2)}) async-start(), calls=%async_computation.11 | async-start | bytes 2359296 | tf_op jit(solution)/shard_map/all_gather | solution.py:41
  248.2 205.1 %all-gather.3.cloned.1.call-start = ((), (), s32[]{:S(2)}) async-start(), calls=%async_computation.9 | async-start | bytes 2359296 | tf_op jit(solution)/shard_map/all_gather | solution.py:41
  318.7 20.1 %copy-start.2 = (s32[256]{0:T(256)S(1)}, s32[256]{0:T(256)}, u32[]{:S(2)}) copy-start(s32[256]{0:T(256)} %param.8) | copy-start | bytes 3076
Sparse Core Ops, SparseCore 0:
  12.1 98.3 reduce-scatter.7
  115.1 91.0 reduce-scatter.5
  210.2 92.4 reduce-scatter.3
  306.1 71.9 all-gather.4
  381.5 71.7 all-gather.2

commit v2 on v1

v2 whole, which is shorter than its diff:
```python
import jax
import jax.numpy as jnp
from jax import lax
from jax.sharding import PartitionSpec as P

RADIUS = 20
HP = lax.Precision.HIGHEST
RING = 4


def smoothing_matrix(count):
    cells = jnp.arange(count, dtype=jnp.int32)
    offset = (cells[:, None] - cells[None, :]).astype(jnp.float32)
    inside = jnp.abs(offset) <= RADIUS
    weights = jnp.where(inside, jnp.exp(-offset * offset / 200.0), jnp.float32(0.0))
    return weights / jnp.sum(weights, axis=1, keepdims=True)


def ring_pairs(n_shots, step):
    hi = n_shots // RING
    return [(h * RING + r, h * RING + (r + step) % RING) for h in range(hi) for r in range(RING)]


def hi_pairs(n_shots):
    hi = n_shots // RING
    return [(h * RING + r, ((h + 1) % hi) * RING + r) for h in range(hi) for r in range(RING)]


def rows(field, start, size):
    return lax.dynamic_slice_in_dim(field, start, size, axis=1)


def reduce_scatter_shots(fields, n_shots):
    idx = lax.axis_index("shots")
    r, h = idx % RING, idx // RING
    chunk = fields[0].shape[1] // RING
    half = chunk // 2
    fwd, bwd = ring_pairs(n_shots, 1), ring_pairs(n_shots, -1)
    acc_f = [rows(f, ((r - 1) % RING) * chunk + h * half, half) for f in fields]
    acc_b = [rows(f, ((r + 1) % RING) * chunk + (1 - h) * half, half) for f in fields]
    for t in range(1, RING):
        recv_f = lax.ppermute(acc_f, "shots", fwd)
        recv_b = lax.ppermute(acc_b, "shots", bwd)
        acc_f = [x + rows(f, ((r - 1 - t) % RING) * chunk + h * half, half) for x, f in zip(recv_f, fields)]
        acc_b = [x + rows(f, ((r + 1 + t) % RING) * chunk + (1 - h) * half, half) for x, f in zip(recv_b, fields)]
    other = lax.ppermute(acc_b, "shots", hi_pairs(n_shots))
    return [a + b for a, b in zip(acc_f, other)]


def all_gather_shots(blocks, n_shots, total):
    idx = lax.axis_index("shots")
    r, h = idx % RING, idx // RING
    chunk = total // RING
    half = chunk // 2
    fwd, bwd = ring_pairs(n_shots, 1), ring_pairs(n_shots, -1)
    outs = [jnp.zeros(b.shape[:1] + (total,) + b.shape[2:], b.dtype) for b in blocks]

    def place(outs, pieces, start):
        return [lax.dynamic_update_slice_in_dim(o, p, start, axis=1) for o, p in zip(outs, pieces)]

    cur_f = list(blocks)
    cur_b = lax.ppermute(cur_f, "shots", hi_pairs(n_shots))
    outs = place(outs, cur_f, r * chunk + h * half)
    outs = place(outs, cur_b, r * chunk + (1 - h) * half)
    for t in range(1, RING):
        cur_f = lax.ppermute(cur_f, "shots", fwd)
        cur_b = lax.ppermute(cur_b, "shots", bwd)
        outs = place(outs, cur_f, ((r - t) % RING) * chunk + h * half)
        outs = place(outs, cur_b, ((r + t) % RING) * chunk + (1 - h) * half)
    return outs


def smooth_depth(field):
    matrix = smoothing_matrix(field.shape[-1])
    return jnp.einsum("...j,ij->...i", field, matrix, precision=HP)


def smooth_across(field):
    matrix = smoothing_matrix(field.shape[1])
    return jnp.einsum("ij,xjz->xiz", matrix, field, precision=HP)


def smooth_along_x(both):
    cols = lax.all_to_all(both, "slab", split_axis=2, concat_axis=1, tiled=True)
    matrix = smoothing_matrix(cols.shape[1])
    cols = jnp.einsum("ij,fjyz->fiyz", matrix, cols, precision=HP)
    return lax.all_to_all(cols, "slab", split_axis=1, concat_axis=2, tiled=True)


def make_body(n_shots):
    def body(vel_parts, den_parts, illum_parts, layer_index, depth_scale):
        total = vel_parts.shape[2]
        vel, den, illum = reduce_scatter_shots(
            [vel_parts[0], den_parts[0], illum_parts[0]], n_shots
        )
        both = jnp.stack([vel / illum, den / illum])
        both = smooth_along_x(smooth_depth(both))
        vel, den = all_gather_shots([both[0], both[1]], n_shots, total)
        vel = smooth_across(vel)
        den = smooth_across(den)
        onehot = (
            layer_index[:, None] == jnp.arange(depth_scale.shape[1], dtype=jnp.int32)[None, :]
        ).astype(jnp.float32)
        per_depth = jnp.dot(depth_scale, onehot.T, precision=HP)
        vel_update = per_depth[0][None, None, :] * vel
        den_update = per_depth[1][None, None, :] * den
        return (vel_update, den_update)

    return body


def solution(mesh):
    placed = (
        P("shots", "slab", None, None),
        P("shots", "slab", None, None),
        P("shots", "slab", None, None),
        P(),
        P(),
    )
    return jax.shard_map(
        make_body(mesh.shape["shots"]),
        mesh=mesh,
        in_specs=placed,
        out_specs=(P("slab", None, None), P("slab", None, None)),
        check_vma=False,
    )
```

time: 471 us -> 295 us (0.63)
  the two profiles are of different devices: /device:TPU:2 before, /device:TPU:8 now
where the time goes in v2:
time: 295 us; the launch traced here: 291 us
  starting transfers between devices  87.3 us (30%)
  waiting for transfers between devices  80.1 us (27%)
  local copies, waits for them, and re-layouts  74.6 us (25%)
  blocking collectives  20.4 us (7%)
  matrix products  14 us (5%)
  other arithmetic  13.1 us (4%)
    dynamic_update_slice x16, local copies, waits for them, and re-layouts, place(): lax.dynamic_update_slice_in_dim(o, p, start, axis=1)  48.9 us
    ppermute x3, waiting for transfers between devices, reduce_scatter_shots(): other = lax.ppermute(acc_b, 'shots', hi_pairs(n_shots))  23.3 us
    all_to_all x1, blocking collectives, smooth_along_x(): return lax.all_to_all(cols, 'slab', split_axis=1, concat_axis=2, tiled=True)  20.4 us
    ppermute x9, starting transfers between devices, reduce_scatter_shots(): recv_f = lax.ppermute(acc_f, 'shots', fwd)  19.5 us
    ppermute x9, starting transfers between devices, reduce_scatter_shots(): recv_b = lax.ppermute(acc_b, 'shots', bwd)  17.5 us
    ppermute x6, starting transfers between devices, all_gather_shots(): cur_b = lax.ppermute(cur_b, 'shots', bwd)  16.2 us
    ppermute x2, waiting for transfers between devices, all_gather_shots(): cur_b = lax.ppermute(cur_f, 'shots', hi_pairs(n_shots))  16.1 us
    all_to_all x1, waiting for transfers between devices, smooth_along_x(): cols = lax.all_to_all(both, 'slab', split_axis=2, concat_axis=1, tiled=True)  15.8 us
  transfers between devices with their start and end apart: 36, of which 17 were waited for; matrix products, arithmetic and copies ran while one was open for 29% of the time, Pallas kernels for 0%

profile of v2, /device:TPU:8, one launch (start us, length us, event | category | flops | bytes accessed | tf_op | source)
XLA Modules:
  0.0 290.7 jit_solution(270761549845924733)
XLA Ops:
  1.9 1.7 collective-permute-start.14
  5.4 1.4 collective-permute-start.7
  6.8 1.9 collective-permute-start.10
  9.6 1.9 collective-permute-done.14
  11.5 2.1 collective-permute-start.3
  14.7 2.5 collective-permute-done.7
  17.1 1.4 collective-permute-start.15
  19.6 3.2 %collective-permute-done = f32[4,64,256]{2,1,0:T(8,128)} collective-permute-done((f32[4,64,256]{2,1,0:T(8,128)}, f32[4,64,256]{2,1,0:T(8,128)}, u32[]{:S(2)}, u32[]{:S(2)}) %collective-permute-start) | collective-permute-done | bytes 262176 | tf_op jit(solution)/shard_map/ppermute | solution.py:42
  26.5 1.8 collective-permute-done.15
  29.4 2.1 collective-permute-start.18
  31.6 2.3 collective-permute-done.8
  33.9 1.7 bitcast_add_fusion.10
  35.6 2.1 collective-permute-start.11
  37.7 1.8 collective-permute-done.1
  40.3 2.1 collective-permute-start.4
  42.3 12.2 %collective-permute-start.2 = (f32[4,64,256]{2,1,0:T(8,128)}, f32[4,64,256]{2,1,0:T(8,128)S(1)}, u32[]{:S(2)}, u32[]{:S(2)}) collective-permute-start(f32[4,64,256]{2,1,0:T(8,128)} %get-tuple-element.10), channel_id=1, source_target_pairs={{0,32},{32,64},{64,96},{96,0},{128,160},{160,192},{192,224},{224,1... | collective-permute-start | bytes 786440 | tf_op jit(solution)/shard_map/ppermute | solution.py:42
  55.6 2.1 collective-permute-start.19
  57.7 2.5 collective-permute-start.12
  60.2 4.7 %collective-permute-done.19 = f32[4,64,256]{2,1,0:T(8,128)S(1)} collective-permute-done((f32[4,64,256]{2,1,0:T(8,128)S(1)}, f32[4,64,256]{2,1,0:T(8,128)S(1)}, u32[]{:S(2)}, u32[]{:S(2)}) %collective-permute-start.19) | collective-permute-done | bytes 262176 | tf_op jit(solution)/shard_map/ppermute | solution.py:43
  64.9 2.0 collective-permute-start.5
  66.9 1.7 bitcast_add_fusion
  69.1 7.4 %collective-permute-start.20 = (f32[4,64,256]{2,1,0:T(8,128)}, f32[4,64,256]{2,1,0:T(8,128)S(1)}, u32[]{:S(2)}, u32[]{:S(2)}) collective-permute-start(f32[4,64,256]{2,1,0:T(8,128)} %bitcast_add_fusion), channel_id=1, source_target_pairs={{0,128},{32,160},{64,192},{96,224},{128,0},{160,32},{192,64},{224,... | collective-permute-start | bytes 786440 | tf_op jit(solution)/shard_map/ppermute | solution.py:46
  77.3 2.0 collective-permute-start.13
  80.1 3.9 %collective-permute-start.6 = (f32[4,64,256]{2,1,0:T(8,128)}, f32[4,64,256]{2,1,0:T(8,128)}, u32[]{:S(2)}, u32[]{:S(2)}) collective-permute-start(f32[4,64,256]{2,1,0:T(8,128)} %bitcast_add_fusion.12), channel_id=1, source_target_pairs={{0,128},{32,160},{64,192},{96,224},{128,0},{160,32},{192,64},{224,... | collective-permute-start | bytes 786440 | tf_op jit(solution)/shard_map/ppermute | solution.py:46
  84.2 8.8 %collective-permute-done.20 = f32[4,64,256]{2,1,0:T(8,128)S(1)} collective-permute-done((f32[4,64,256]{2,1,0:T(8,128)}, f32[4,64,256]{2,1,0:T(8,128)S(1)}, u32[]{:S(2)}, u32[]{:S(2)}) %collective-permute-start.20) | collective-permute-done | bytes 262176 | tf_op jit(solution)/shard_map/ppermute | solution.py:46
  93.0 10.9 %collective-permute-done.13 = f32[4,64,256]{2,1,0:T(8,128)S(1)} collective-permute-done((f32[4,64,256]{2,1,0:T(8,128)}, f32[4,64,256]{2,1,0:T(8,128)S(1)}, u32[]{:S(2)}, u32[]{:S(2)}) %collective-permute-start.13) | collective-permute-done | bytes 262176 | tf_op jit(solution)/shard_map/ppermute | solution.py:46
  103.9 3.6 %collective-permute-done.6 = f32[4,64,256]{2,1,0:T(8,128)} collective-permute-done((f32[4,64,256]{2,1,0:T(8,128)}, f32[4,64,256]{2,1,0:T(8,128)}, u32[]{:S(2)}, u32[]{:S(2)}) %collective-permute-start.6) | collective-permute-done | bytes 262176 | tf_op jit(solution)/shard_map/ppermute | solution.py:46
  110.7 5.6 %all-to-all-start = ((f32[2,4,64,256]{3,1,0,2:T(4,128)}), f32[2,4,64,256]{3,1,0,2:T(4,128)S(1)}, u32[]{:S(2)}, u32[]{:S(2)}) async-start(f32[2,4,64,256]{3,1,0,2:T(4,128)} %copy.35), calls=%async_computation | async-start | bytes 1048576 | tf_op jit(solution)/shard_map/all_to_all | solution.py:84
  116.4 15.8 %all-to-all-done = f32[2,4,64,256]{3,1,0,2:T(4,128)S(1)} async-done(((f32[2,4,64,256]{3,1,0,2:T(4,128)}), f32[2,4,64,256]{3,1,0,2:T(4,128)S(1)}, u32[]{:S(2)}, u32[]{:S(2)}) %all-to-all-start) | async-done | bytes 524320 | tf_op jit(solution)/shard_map/all_to_all | solution.py:84
  133.8 20.4 %all_to_all.33 = f32[2,128,2,256]{3,2,0,1:T(2,128)S(1)} all-to-all(f32[2,128,2,256]{3,2,0,1:T(2,128)S(1)} %copy.38), channel_id=1, replica_groups=mesh['shots'=8,'slab'=32] {'slab'}, dimensions={1} | all-to-all | bytes 1048576 | tf_op jit(solution)/shard_map/all_to_all | solution.py:87
  154.6 3.2 %collective-permute-start.28 = (f32[4,64,256]{2,0,1:T(4,128)S(1)}, f32[4,64,256]{2,0,1:T(4,128)S(1)}, u32[]{:S(2)}, u32[]{:S(2)}) collective-permute-start(f32[4,64,256]{2,0,1:T(4,128)S(1)} %bitcast.110), channel_id=1, source_target_pairs={{0,128},{32,160},{64,192},{96,224},{128,0},{160,32},{192,64},{224,... | collective-permute-start | bytes 786440 | tf_op jit(solution)/shard_map/ppermute | solution.py:62
  157.7 2.5 collective-permute-start.29
  160.3 2.9 %collective-permute-start.21 = (f32[4,64,256]{2,0,1:T(4,128)S(1)}, f32[4,64,256]{2,0,1:T(4,128)S(1)}, u32[]{:S(2)}, u32[]{:S(2)}) collective-permute-start(f32[4,64,256]{2,0,1:T(4,128)S(1)} %bitcast.113), channel_id=1, source_target_pairs={{0,128},{32,160},{64,192},{96,224},{128,0},{160,32},{192,64},{224,... | collective-permute-start | bytes 786440 | tf_op jit(solution)/shard_map/ppermute | solution.py:62
  163.2 2.7 collective-permute-start.22
  165.9 10.2 %collective-permute-done.28 = f32[4,64,256]{2,0,1:T(4,128)S(1)} collective-permute-done((f32[4,64,256]{2,0,1:T(4,128)S(1)}, f32[4,64,256]{2,0,1:T(4,128)S(1)}, u32[]{:S(2)}, u32[]{:S(2)}) %collective-permute-start.28) | collective-permute-done | bytes 262176 | tf_op jit(solution)/shard_map/ppermute | solution.py:62
  176.1 2.5 collective-permute-start.31
  178.7 5.9 %collective-permute-done.21 = f32[4,64,256]{2,0,1:T(4,128)S(1)} collective-permute-done((f32[4,64,256]{2,0,1:T(4,128)S(1)}, f32[4,64,256]{2,0,1:T(4,128)S(1)}, u32[]{:S(2)}, u32[]{:S(2)}) %collective-permute-start.21) | collective-permute-done | bytes 262176 | tf_op jit(solution)/shard_map/ppermute | solution.py:62
  187.1 3.3 %collective-permute-start.32 = (f32[4,64,256]{2,0,1:T(4,128)S(1)}, f32[4,64,256]{2,0,1:T(4,128)S(1)}, u32[]{:S(2)}, u32[]{:S(2)}) collective-permute-start(f32[4,64,256]{2,0,1:T(4,128)S(1)} %collective-permute-done.30), channel_id=1, source_target_pairs={{0,96},{32,0},{64,32},{96,64},{128,224},{160,128},{192,160},{224,1... | collective-permute-start | bytes 786440 | tf_op jit(solution)/shard_map/ppermute | solution.py:67
  190.7 3.5 %collective-permute-done.23 = f32[4,64,256]{2,0,1:T(4,128)S(1)} collective-permute-done((f32[4,64,256]{2,0,1:T(4,128)S(1)}, f32[4,64,256]{2,0,1:T(4,128)S(1)}, u32[]{:S(2)}, u32[]{:S(2)}) %collective-permute-start.23) | collective-permute-done | bytes 262176 | tf_op jit(solution)/shard_map/ppermute | solution.py:67
  194.1 2.9 collective-permute-start.25
  197.5 2.3 collective-permute-done.32
  199.8 3.2 %collective-permute-start.34 = (f32[4,64,256]{2,0,1:T(4,128)S(1)}, f32[4,64,256]{2,0,1:T(4,128)}, u32[]{:S(2)}, u32[]{:S(2)}) collective-permute-start(f32[4,64,256]{2,0,1:T(4,128)S(1)} %collective-permute-done.32), channel_id=1, source_target_pairs={{0,96},{32,0},{64,32},{96,64},{128,224},{160,128},{192,160},{224,1... | collective-permute-start | bytes 786440 | tf_op jit(solution)/shard_map/ppermute | solution.py:67
  203.9 1.6 broadcast.30.clone.1
  205.5 3.4 %dynamic_update_slice.56 = f32[4,512,256]{1,2,0:T(8,128)} dynamic-update-slice(f32[4,512,256]{1,2,0:T(8,128)} %broadcast.30.clone.1, f32[4,64,256]{1,2,0:T(8,128)S(1)} %copy.50, s32[]{:T(128)} %constant.163.clone.1, s32[]{:T(128)S(6)} %select_n.189, s32[]{:T(128)} %constant.163.clone.1) | dynamic-update-slice | bytes 524292 | tf_op jit(solution)/shard_map/dynamic_update_slice | solution.py:59
  209.2 2.3 dynamic_update_slice.48
  212.7 4.0 %dynamic_update_slice.57 = f32[4,512,256]{1,2,0:T(8,128)} dynamic-update-slice(f32[4,512,256]{1,2,0:T(8,128)} %dynamic_update_slice.56, f32[4,64,256]{1,2,0:T(8,128)S(1)} %copy.51, s32[]{:T(128)} %constant.163.clone.1, s32[]{:T(128)S(6)} %select_n.190, s32[]{:T(128)} %constant.163.clone.1) | dynamic-update-slice | bytes 524292 | tf_op jit(solution)/shard_map/dynamic_update_slice | solution.py:59
  217.8 3.4 %dynamic_update_slice.58 = f32[4,512,256]{1,2,0:T(8,128)} dynamic-update-slice(f32[4,512,256]{1,2,0:T(8,128)} %dynamic_update_slice.57, f32[4,64,256]{1,2,0:T(8,128)S(1)} %copy.52, s32[]{:T(128)} %constant.163.clone.1, s32[]{:T(128)S(6)} %select_n.172, s32[]{:T(128)} %constant.163.clone.1) | dynamic-update-slice | bytes 524292 | tf_op jit(solution)/shard_map/dynamic_update_slice | solution.py:59
  222.4 3.3 %dynamic_update_slice.49 = f32[4,512,256]{1,2,0:T(8,128)S(1)} dynamic-update-slice(f32[4,512,256]{1,2,0:T(8,128)S(1)} %dynamic_update_slice.48, f32[4,64,256]{1,2,0:T(8,128)S(1)} %copy.42, s32[]{:T(128)} %constant.163.clone.1, s32[]{:T(128)S(6)} %select_n.190, s32[]{:T(128)} %constant.163.clone.1) | dynamic-update-slice | bytes 524292 | tf_op jit(solution)/shard_map/dynamic_update_slice | solution.py:59
  226.9 2.3 dynamic_update_slice.50
  230.3 4.0 %dynamic_update_slice.59 = f32[4,512,256]{1,2,0:T(8,128)} dynamic-update-slice(f32[4,512,256]{1,2,0:T(8,128)} %dynamic_update_slice.58, f32[4,64,256]{1,2,0:T(8,128)S(1)} %copy.53, s32[]{:T(128)} %constant.163.clone.1, s32[]{:T(128)S(6)} %select_n.180, s32[]{:T(128)} %constant.163.clone.1) | dynamic-update-slice | bytes 524292 | tf_op jit(solution)/shard_map/dynamic_update_slice | solution.py:59
  235.4 2.8 dynamic_update_slice.60
  238.5 3.3 %dynamic_update_slice.51 = f32[4,512,256]{1,2,0:T(8,128)S(1)} dynamic-update-slice(f32[4,512,256]{1,2,0:T(8,128)S(1)} %dynamic_update_slice.50, f32[4,64,256]{1,2,0:T(8,128)S(1)} %copy.44, s32[]{:T(128)} %constant.163.clone.1, s32[]{:T(128)S(6)} %select_n.180, s32[]{:T(128)} %constant.163.clone.1) | dynamic-update-slice | bytes 524292 | tf_op jit(solution)/shard_map/dynamic_update_slice | solution.py:59
  242.0 1.4 dynamic_update_slice.52
  243.6 3.4 %dynamic_update_slice.61 = f32[4,512,256]{1,2,0:T(8,128)} dynamic-update-slice(f32[4,512,256]{1,2,0:T(8,128)} %dynamic_update_slice.60, f32[4,64,256]{1,2,0:T(8,128)S(1)} %copy.55, s32[]{:T(128)} %constant.163.clone.1, s32[]{:T(128)S(6)} %select_n.182, s32[]{:T(128)} %constant.163.clone.1) | dynamic-update-slice | bytes 524292 | tf_op jit(solution)/shard_map/dynamic_update_slice | solution.py:59
  248.2 3.4 %dynamic_update_slice.62 = f32[4,512,256]{1,2,0:T(8,128)} dynamic-update-slice(f32[4,512,256]{1,2,0:T(8,128)} %dynamic_update_slice.61, f32[4,64,256]{1,2,0:T(8,128)S(1)} %copy.56, s32[]{:T(128)} %constant.163.clone.1, s32[]{:T(128)S(6)} %select_n.176, s32[]{:T(128)} %constant.163.clone.1) | dynamic-update-slice | bytes 524292 | tf_op jit(solution)/shard_map/dynamic_update_slice | solution.py:59
  252.8 2.4 dynamic_update_slice.53
  256.3 2.3 dynamic_update_slice.54
  258.6 5.4 %collective-permute-start.27 = (f32[4,64,256]{2,0,1:T(4,128)}, f32[4,64,256]{2,0,1:T(4,128)S(1)}, u32[]{:S(2)}, u32[]{:S(2)}) collective-permute-start(f32[4,64,256]{2,0,1:T(4,128)} %collective-permute-done.25), channel_id=1, source_target_pairs={{0,96},{32,0},{64,32},{96,64},{128,224},{160,128},{192,160},{224,1... | collective-permute-start | bytes 786440 | tf_op jit(solution)/shard_map/ppermute | solution.py:67
  265.2 4.0 %dynamic_update_slice.63 = f32[4,512,256]{1,2,0:T(8,128)} dynamic-update-slice(f32[4,512,256]{1,2,0:T(8,128)} %dynamic_update_slice.62, f32[4,64,256]{1,2,0:T(8,128)S(1)} %copy.57, s32[]{:T(128)} %constant.163.clone.1, s32[]{:T(128)S(6)} %select_n.184, s32[]{:T(128)} %constant.163.clone.1) | dynamic-update-slice | bytes 524292 | tf_op jit(solution)/shard_map/dynamic_update_slice | solution.py:59
  269.2 6.8 %multiply_bitcast_fusion = f32[4,512,256]{1,2,0:T(8,128)} fusion(f32[4,512,256]{1,2,0:T(8,128)} %dynamic_update_slice.63, f32[256]{0:T(256)S(1)} %bitcast.117, f32[512]{0:T(512)S(1)} %fusion.6), kind=kOutput, calls=%fused_computation | convolution fusion | flops 3224109056 | bytes 4197376 | tf_op jit(solution)/shard_map/ij,xjz->xiz/dot_general | solution.py:80
  276.0 2.9 copy.59
  279.1 3.3 %dynamic_update_slice.55 = f32[4,512,256]{1,2,0:T(8,128)S(1)} dynamic-update-slice(f32[4,512,256]{1,2,0:T(8,128)S(1)} %dynamic_update_slice.54, f32[4,64,256]{1,2,0:T(8,128)S(1)} %copy.48, s32[]{:T(128)} %constant.163.clone.1, s32[]{:T(128)S(6)} %select_n.184, s32[]{:T(128)} %constant.163.clone.1) | dynamic-update-slice | bytes 524292 | tf_op jit(solution)/shard_map/dynamic_update_slice | solution.py:59
  282.4 5.2 %multiply_bitcast_fusion.1 = f32[4,512,256]{1,2,0:T(8,128)} fusion(f32[4,512,256]{1,2,0:T(8,128)S(1)} %dynamic_update_slice.55, f32[256]{0:T(256)S(1)} %bitcast.116, f32[512]{0:T(512)S(1)} %fusion.6), kind=kOutput, calls=%fused_computation.1 | convolution fusion | flops 3224109056 | bytes 4197376 | tf_op jit(solution)/shard_map/ij,xjz->xiz/dot_general | solution.py:80
  287.6 2.9 copy.58
  (95 shorter events, 37.1 us)
Async XLA Ops:
  0.6 189.8 %copy-start = (f32[2,16]{1,0:T(2,128)S(1)}, f32[2,16]{1,0:T(2,128)}, u32[]{:S(2)}) copy-start(f32[2,16]{1,0:T(2,128)} %param.9) | copy-start | bytes 388
  0.6 8.1 %copy-start.1 = (f32[1,4,512,256]{3,2,1,0:T(8,128)S(1)}, f32[1,4,512,256]{3,2,1,0:T(8,128)}, u32[]{:S(2)}) copy-start(f32[1,4,512,256]{3,2,1,0:T(8,128)} %param.5) | copy-start | bytes 6291460
  1.9 9.6 %collective-permute-start.14 = (f32[4,64,256]{2,1,0:T(8,128)S(1)}, f32[4,64,256]{2,1,0:T(8,128)}, u32[]{:S(2)}, u32[]{:S(2)}) collective-permute-start(f32[4,64,256]{2,1,0:T(8,128)S(1)} %get-tuple-element.20), channel_id=1, source_target_pairs={{0,32},{32,64},{64,96},{96,0},{128,160},{160,192},{192,224},{224,1... | collective-permute-start | bytes 786440 | tf_op jit(solution)/shard_map/ppermute | solution.py:42
  3.6 21.5 %collective-permute-start.17 = (f32[4,64,256]{2,1,0:T(8,128)S(1)}, f32[4,64,256]{2,1,0:T(8,128)}, u32[]{:S(2)}, u32[]{:S(2)}) collective-permute-start(f32[4,64,256]{2,1,0:T(8,128)S(1)} %get-tuple-element.21), channel_id=1, source_target_pairs={{0,96},{32,0},{64,32},{96,64},{128,224},{160,128},{192,160},{224,1... | collective-permute-start | bytes 786440 | tf_op jit(solution)/shard_map/ppermute | solution.py:43
  5.4 11.7 %collective-permute-start.7 = (f32[4,64,256]{2,1,0:T(8,128)S(1)}, f32[4,64,256]{2,1,0:T(8,128)}, u32[]{:S(2)}, u32[]{:S(2)}) collective-permute-start(f32[4,64,256]{2,1,0:T(8,128)S(1)} %get-tuple-element.16), channel_id=1, source_target_pairs={{0,32},{32,64},{64,96},{96,0},{128,160},{160,192},{192,224},{224,1... | collective-permute-start | bytes 786440 | tf_op jit(solution)/shard_map/ppermute | solution.py:42
  6.8 24.8 %collective-permute-start.10 = (f32[4,64,256]{2,1,0:T(8,128)S(1)}, f32[4,64,256]{2,1,0:T(8,128)}, u32[]{:S(2)}, u32[]{:S(2)}) collective-permute-start(f32[4,64,256]{2,1,0:T(8,128)S(1)} %get-tuple-element.17), channel_id=1, source_target_pairs={{0,96},{32,0},{64,32},{96,64},{128,224},{160,128},{192,160},{224,1... | collective-permute-start | bytes 786440 | tf_op jit(solution)/shard_map/ppermute | solution.py:43
  9.4 13.3 %collective-permute-start = (f32[4,64,256]{2,1,0:T(8,128)}, f32[4,64,256]{2,1,0:T(8,128)}, u32[]{:S(2)}, u32[]{:S(2)}) collective-permute-start(f32[4,64,256]{2,1,0:T(8,128)} %get-tuple-element.12), channel_id=1, source_target_pairs={{0,32},{32,64},{64,96},{96,0},{128,160},{160,192},{192,224},{224,1... | collective-permute-start | bytes 786440 | tf_op jit(solution)/shard_map/ppermute | solution.py:42
  9.6 24.3 %copy-start.2 = (f32[1,4,512,256]{3,2,1,0:T(8,128)S(1)}, f32[1,4,512,256]{3,2,1,0:T(8,128)}, u32[]{:S(2)}) copy-start(f32[1,4,512,256]{3,2,1,0:T(8,128)} %param.7) | copy-start | bytes 6291460
  11.5 26.2 %collective-permute-start.3 = (f32[4,64,256]{2,1,0:T(8,128)S(1)}, f32[4,64,256]{2,1,0:T(8,128)S(1)}, u32[]{:S(2)}, u32[]{:S(2)}) collective-permute-start(f32[4,64,256]{2,1,0:T(8,128)S(1)} %get-tuple-element.13), channel_id=1, source_target_pairs={{0,96},{32,0},{64,32},{96,64},{128,224},{160,128},{192,160},{224,1... | collective-permute-start | bytes 786440 | tf_op jit(solution)/shard_map/ppermute | solution.py:43
  17.1 11.1 %collective-permute-start.15 = (f32[4,64,256]{2,1,0:T(8,128)S(1)}, f32[4,64,256]{2,1,0:T(8,128)S(1)}, u32[]{:S(2)}, u32[]{:S(2)}) collective-permute-start(f32[4,64,256]{2,1,0:T(8,128)S(1)} %bitcast_add_fusion.5), channel_id=1, source_target_pairs={{0,32},{32,64},{64,96},{96,0},{128,160},{160,192},{192,224},{224,1... | collective-permute-start | bytes 786440 | tf_op jit(solution)/shard_map/ppermute | solution.py:42
  22.7 11.1 %collective-permute-start.8 = (f32[4,64,256]{2,1,0:T(8,128)S(1)}, f32[4,64,256]{2,1,0:T(8,128)S(1)}, u32[]{:S(2)}, u32[]{:S(2)}) collective-permute-start(f32[4,64,256]{2,1,0:T(8,128)S(1)} %bitcast_add_fusion.11), channel_id=1, source_target_pairs={{0,32},{32,64},{64,96},{96,0},{128,160},{160,192},{192,224},{224,1... | collective-permute-start | bytes 786440 | tf_op jit(solution)/shard_map/ppermute | solution.py:42
  25.1 14.4 %collective-permute-start.1 = (f32[4,64,256]{2,1,0:T(8,128)S(1)}, f32[4,64,256]{2,1,0:T(8,128)S(1)}, u32[]{:S(2)}, u32[]{:S(2)}) collective-permute-start(f32[4,64,256]{2,1,0:T(8,128)S(1)} %bitcast_add_fusion.17), channel_id=1, source_target_pairs={{0,32},{32,64},{64,96},{96,0},{128,160},{160,192},{192,224},{224,1... | collective-permute-start | bytes 786440 | tf_op jit(solution)/shard_map/ppermute | solution.py:42
  29.4 12.9 %collective-permute-start.18 = (f32[4,64,256]{2,1,0:T(8,128)S(1)}, f32[4,64,256]{2,1,0:T(8,128)S(1)}, u32[]{:S(2)}, u32[]{:S(2)}) collective-permute-start(f32[4,64,256]{2,1,0:T(8,128)S(1)} %get-tuple-element.19), channel_id=1, source_target_pairs={{0,96},{32,0},{64,32},{96,64},{128,224},{160,128},{192,160},{224,1... | collective-permute-start | bytes 786440 | tf_op jit(solution)/shard_map/ppermute | solution.py:43
  31.6 48.5 %collective-permute-start.16 = (f32[4,64,256]{2,1,0:T(8,128)S(1)}, f32[4,64,256]{2,1,0:T(8,128)S(1)}, u32[]{:S(2)}, u32[]{:S(2)}) collective-permute-start(f32[4,64,256]{2,1,0:T(8,128)S(1)} %get-tuple-element.18), channel_id=1, source_target_pairs={{0,32},{32,64},{64,96},{96,0},{128,160},{160,192},{192,224},{224,1... | collective-permute-start | bytes 786440 | tf_op jit(solution)/shard_map/ppermute | solution.py:42
  35.6 20.0 %collective-permute-start.11 = (f32[4,64,256]{2,1,0:T(8,128)S(1)}, f32[4,64,256]{2,1,0:T(8,128)S(1)}, u32[]{:S(2)}, u32[]{:S(2)}) collective-permute-start(f32[4,64,256]{2,1,0:T(8,128)S(1)} %get-tuple-element.15), channel_id=1, source_target_pairs={{0,96},{32,0},{64,32},{96,64},{128,224},{160,128},{192,160},{224,1... | collective-permute-start | bytes 786440 | tf_op jit(solution)/shard_map/ppermute | solution.py:43
  37.7 46.5 %collective-permute-start.9 = (f32[4,64,256]{2,1,0:T(8,128)}, f32[4,64,256]{2,1,0:T(8,128)S(1)}, u32[]{:S(2)}, u32[]{:S(2)}) collective-permute-start(f32[4,64,256]{2,1,0:T(8,128)} %get-tuple-element.14), channel_id=1, source_target_pairs={{0,32},{32,64},{64,96},{96,0},{128,160},{160,192},{192,224},{224,1... | collective-permute-start | bytes 786440 | tf_op jit(solution)/shard_map/ppermute | solution.py:42
  40.3 17.4 %collective-permute-start.4 = (f32[4,64,256]{2,1,0:T(8,128)S(1)}, f32[4,64,256]{2,1,0:T(8,128)S(1)}, u32[]{:S(2)}, u32[]{:S(2)}) collective-permute-start(f32[4,64,256]{2,1,0:T(8,128)S(1)} %get-tuple-element.11), channel_id=1, source_target_pairs={{0,96},{32,0},{64,32},{96,64},{128,224},{160,128},{192,160},{224,1... | collective-permute-start | bytes 786440 | tf_op jit(solution)/shard_map/ppermute | solution.py:43
  42.3 41.8 %collective-permute-start.2 = (f32[4,64,256]{2,1,0:T(8,128)}, f32[4,64,256]{2,1,0:T(8,128)S(1)}, u32[]{:S(2)}, u32[]{:S(2)}) collective-permute-start(f32[4,64,256]{2,1,0:T(8,128)} %get-tuple-element.10), channel_id=1, source_target_pairs={{0,32},{32,64},{64,96},{96,0},{128,160},{160,192},{192,224},{224,1... | collective-permute-start | bytes 786440 | tf_op jit(solution)/shard_map/ppermute | solution.py:42
  55.6 9.3 %collective-permute-start.19 = (f32[4,64,256]{2,1,0:T(8,128)S(1)}, f32[4,64,256]{2,1,0:T(8,128)S(1)}, u32[]{:S(2)}, u32[]{:S(2)}) collective-permute-start(f32[4,64,256]{2,1,0:T(8,128)S(1)} %bitcast_add_fusion.1), channel_id=1, source_target_pairs={{0,96},{32,0},{64,32},{96,64},{128,224},{160,128},{192,160},{224,1... | collective-permute-start | bytes 786440 | tf_op jit(solution)/shard_map/ppermute | solution.py:43
  57.7 11.4 %collective-permute-start.12 = (f32[4,64,256]{2,1,0:T(8,128)S(1)}, f32[4,64,256]{2,1,0:T(8,128)S(1)}, u32[]{:S(2)}, u32[]{:S(2)}) collective-permute-start(f32[4,64,256]{2,1,0:T(8,128)S(1)} %bitcast_add_fusion.7), channel_id=1, source_target_pairs={{0,96},{32,0},{64,32},{96,64},{128,224},{160,128},{192,160},{224,1... | collective-permute-start | bytes 786440 | tf_op jit(solution)/shard_map/ppermute | solution.py:43
  64.9 12.4 %collective-permute-start.5 = (f32[4,64,256]{2,1,0:T(8,128)S(1)}, f32[4,64,256]{2,1,0:T(8,128)S(1)}, u32[]{:S(2)}, u32[]{:S(2)}) collective-permute-start(f32[4,64,256]{2,1,0:T(8,128)S(1)} %bitcast_add_fusion.13), channel_id=1, source_target_pairs={{0,96},{32,0},{64,32},{96,64},{128,224},{160,128},{192,160},{224,1... | collective-permute-start | bytes 786440 | tf_op jit(solution)/shard_map/ppermute | solution.py:43
  69.1 23.9 %collective-permute-start.20 = (f32[4,64,256]{2,1,0:T(8,128)}, f32[4,64,256]{2,1,0:T(8,128)S(1)}, u32[]{:S(2)}, u32[]{:S(2)}) collective-permute-start(f32[4,64,256]{2,1,0:T(8,128)} %bitcast_add_fusion), channel_id=1, source_target_pairs={{0,128},{32,160},{64,192},{96,224},{128,0},{160,32},{192,64},{224,... | collective-permute-start | bytes 786440 | tf_op jit(solution)/shard_map/ppermute | solution.py:46
  77.3 26.6 %collective-permute-start.13 = (f32[4,64,256]{2,1,0:T(8,128)}, f32[4,64,256]{2,1,0:T(8,128)S(1)}, u32[]{:S(2)}, u32[]{:S(2)}) collective-permute-start(f32[4,64,256]{2,1,0:T(8,128)} %bitcast_add_fusion.6), channel_id=1, source_target_pairs={{0,128},{32,160},{64,192},{96,224},{128,0},{160,32},{192,64},{224,... | collective-permute-start | bytes 786440 | tf_op jit(solution)/shard_map/ppermute | solution.py:46
  80.1 27.4 %collective-permute-start.6 = (f32[4,64,256]{2,1,0:T(8,128)}, f32[4,64,256]{2,1,0:T(8,128)}, u32[]{:S(2)}, u32[]{:S(2)}) collective-permute-start(f32[4,64,256]{2,1,0:T(8,128)} %bitcast_add_fusion.12), channel_id=1, source_target_pairs={{0,128},{32,160},{64,192},{96,224},{128,0},{160,32},{192,64},{224,... | collective-permute-start | bytes 786440 | tf_op jit(solution)/shard_map/ppermute | solution.py:46
  110.7 21.5 %all-to-all-start = ((f32[2,4,64,256]{3,1,0,2:T(4,128)}), f32[2,4,64,256]{3,1,0,2:T(4,128)S(1)}, u32[]{:S(2)}, u32[]{:S(2)}) async-start(f32[2,4,64,256]{3,1,0,2:T(4,128)} %copy.35), calls=%async_computation | async-start | bytes 1048576 | tf_op jit(solution)/shard_map/all_to_all | solution.py:84
  133.8 56.7 %copy-start.8 = (s32[256]{0:T(256)S(1)}, s32[256]{0:T(256)}, u32[]{:S(2)}) copy-start(s32[256]{0:T(256)} %param.8) | copy-start | bytes 3076
  154.6 21.5 %collective-permute-start.28 = (f32[4,64,256]{2,0,1:T(4,128)S(1)}, f32[4,64,256]{2,0,1:T(4,128)S(1)}, u32[]{:S(2)}, u32[]{:S(2)}) collective-permute-start(f32[4,64,256]{2,0,1:T(4,128)S(1)} %bitcast.110), channel_id=1, source_target_pairs={{0,128},{32,160},{64,192},{96,224},{128,0},{160,32},{192,64},{224,... | collective-permute-start | bytes 786440 | tf_op jit(solution)/shard_map/ppermute | solution.py:62
  157.7 18.4 %collective-permute-start.29 = (f32[4,64,256]{2,0,1:T(4,128)S(1)}, f32[4,64,256]{2,0,1:T(4,128)S(1)}, u32[]{:S(2)}, u32[]{:S(2)}) collective-permute-start(f32[4,64,256]{2,0,1:T(4,128)S(1)} %bitcast.111), channel_id=1, source_target_pairs={{0,32},{32,64},{64,96},{96,0},{128,160},{160,192},{192,224},{224,1... | collective-permute-start | bytes 786440 | tf_op jit(solution)/shard_map/ppermute | solution.py:66
  160.3 24.3 %collective-permute-start.21 = (f32[4,64,256]{2,0,1:T(4,128)S(1)}, f32[4,64,256]{2,0,1:T(4,128)S(1)}, u32[]{:S(2)}, u32[]{:S(2)}) collective-permute-start(f32[4,64,256]{2,0,1:T(4,128)S(1)} %bitcast.113), channel_id=1, source_target_pairs={{0,128},{32,160},{64,192},{96,224},{128,0},{160,32},{192,64},{224,... | collective-permute-start | bytes 786440 | tf_op jit(solution)/shard_map/ppermute | solution.py:62
  163.2 22.7 %collective-permute-start.22 = (f32[4,64,256]{2,0,1:T(4,128)S(1)}, f32[4,64,256]{2,0,1:T(4,128)S(1)}, u32[]{:S(2)}, u32[]{:S(2)}) collective-permute-start(f32[4,64,256]{2,0,1:T(4,128)S(1)} %bitcast.114), channel_id=1, source_target_pairs={{0,32},{32,64},{64,96},{96,0},{128,160},{160,192},{192,224},{224,1... | collective-permute-start | bytes 786440 | tf_op jit(solution)/shard_map/ppermute | solution.py:66
  176.1 29.4 %copy-start.5 = (f32[4,64,256]{2,0,1:T(4,128)}, f32[4,64,256]{2,0,1:T(4,128)S(1)}, u32[]{:S(2)}) copy-start(f32[4,64,256]{2,0,1:T(4,128)S(1)} %collective-permute-done.28) | copy-start | bytes 786436
  176.1 11.0 %collective-permute-start.30 = (f32[4,64,256]{2,0,1:T(4,128)S(1)}, f32[4,64,256]{2,0,1:T(4,128)S(1)}, u32[]{:S(2)}, u32[]{:S(2)}) collective-permute-start(f32[4,64,256]{2,0,1:T(4,128)S(1)} %collective-permute-done.28), channel_id=1, source_target_pairs={{0,96},{32,0},{64,32},{96,64},{128,224},{160,128},{192,160},{224,1... | collective-permute-start | bytes 786440 | tf_op jit(solution)/shard_map/ppermute | solution.py:67
  176.1 27.4 %copy-start.3 = (f32[4,64,256]{2,0,1:T(4,128)}, f32[4,64,256]{2,0,1:T(4,128)S(1)}, u32[]{:S(2)}) copy-start(f32[4,64,256]{2,0,1:T(4,128)S(1)} %collective-permute-done.29) | copy-start | bytes 786436
  176.1 14.5 %collective-permute-start.31 = (f32[4,64,256]{2,0,1:T(4,128)S(1)}, f32[4,64,256]{2,0,1:T(4,128)}, u32[]{:S(2)}, u32[]{:S(2)}) collective-permute-start(f32[4,64,256]{2,0,1:T(4,128)S(1)} %collective-permute-done.29), channel_id=1, source_target_pairs={{0,32},{32,64},{64,96},{96,0},{128,160},{160,192},{192,224},{224,1... | collective-permute-start | bytes 786440 | tf_op jit(solution)/shard_map/ppermute | solution.py:66
  184.6 21.0 %copy-start.7 = (f32[4,64,256]{2,0,1:T(4,128)}, f32[4,64,256]{2,0,1:T(4,128)S(1)}, u32[]{:S(2)}) copy-start(f32[4,64,256]{2,0,1:T(4,128)S(1)} %collective-permute-done.21) | copy-start | bytes 786436
  184.6 9.6 %collective-permute-start.23 = (f32[4,64,256]{2,0,1:T(4,128)S(1)}, f32[4,64,256]{2,0,1:T(4,128)S(1)}, u32[]{:S(2)}, u32[]{:S(2)}) collective-permute-start(f32[4,64,256]{2,0,1:T(4,128)S(1)} %collective-permute-done.21), channel_id=1, source_target_pairs={{0,96},{32,0},{64,32},{96,64},{128,224},{160,128},{192,160},{224,1... | collective-permute-start | bytes 786440 | tf_op jit(solution)/shard_map/ppermute | solution.py:67
  185.9 17.5 %copy-start.4 = (f32[4,64,256]{2,0,1:T(4,128)}, f32[4,64,256]{2,0,1:T(4,128)S(1)}, u32[]{:S(2)}) copy-start(f32[4,64,256]{2,0,1:T(4,128)S(1)} %collective-permute-done.22) | copy-start | bytes 786436
  185.9 11.5 %collective-permute-start.24 = (f32[4,64,256]{2,0,1:T(4,128)S(1)}, f32[4,64,256]{2,0,1:T(4,128)S(1)}, u32[]{:S(2)}, u32[]{:S(2)}) collective-permute-start(f32[4,64,256]{2,0,1:T(4,128)S(1)} %collective-permute-done.22), channel_id=1, source_target_pairs={{0,32},{32,64},{64,96},{96,0},{128,160},{160,192},{192,224},{224,1... | collective-permute-start | bytes 786440 | tf_op jit(solution)/shard_map/ppermute | solution.py:66
  187.1 18.4 %copy-start.6 = (f32[4,64,256]{2,0,1:T(4,128)}, f32[4,64,256]{2,0,1:T(4,128)S(1)}, u32[]{:S(2)}) copy-start(f32[4,64,256]{2,0,1:T(4,128)S(1)} %collective-permute-done.30) | copy-start | bytes 786436
  187.1 12.6 %collective-permute-start.32 = (f32[4,64,256]{2,0,1:T(4,128)S(1)}, f32[4,64,256]{2,0,1:T(4,128)S(1)}, u32[]{:S(2)}, u32[]{:S(2)}) collective-permute-start(f32[4,64,256]{2,0,1:T(4,128)S(1)} %collective-permute-done.30), channel_id=1, source_target_pairs={{0,96},{32,0},{64,32},{96,64},{128,224},{160,128},{192,160},{224,1... | collective-permute-start | bytes 786440 | tf_op jit(solution)/shard_map/ppermute | solution.py:67
  190.6 56.4 %collective-permute-start.33 = (f32[4,64,256]{2,0,1:T(4,128)}, f32[4,64,256]{2,0,1:T(4,128)}, u32[]{:S(2)}, u32[]{:S(2)}) collective-permute-start(f32[4,64,256]{2,0,1:T(4,128)} %collective-permute-done.31), channel_id=1, source_target_pairs={{0,32},{32,64},{64,96},{96,0},{128,160},{160,192},{192,224},{224,1... | collective-permute-start | bytes 786440 | tf_op jit(solution)/shard_map/ppermute | solution.py:66
  194.1 57.5 %collective-permute-start.25 = (f32[4,64,256]{2,0,1:T(4,128)S(1)}, f32[4,64,256]{2,0,1:T(4,128)}, u32[]{:S(2)}, u32[]{:S(2)}) collective-permute-start(f32[4,64,256]{2,0,1:T(4,128)S(1)} %collective-permute-done.23), channel_id=1, source_target_pairs={{0,96},{32,0},{64,32},{96,64},{128,224},{160,128},{192,160},{224,1... | collective-permute-start | bytes 786440 | tf_op jit(solution)/shard_map/ppermute | solution.py:67
  197.5 57.7 %collective-permute-start.26 = (f32[4,64,256]{2,0,1:T(4,128)S(1)}, f32[4,64,256]{2,0,1:T(4,128)}, u32[]{:S(2)}, u32[]{:S(2)}) collective-permute-start(f32[4,64,256]{2,0,1:T(4,128)S(1)} %collective-permute-done.24), channel_id=1, source_target_pairs={{0,32},{32,64},{64,96},{96,0},{128,160},{160,192},{192,224},{224,1... | collective-permute-start | bytes 786440 | tf_op jit(solution)/shard_map/ppermute | solution.py:66
  199.8 64.3 %collective-permute-start.34 = (f32[4,64,256]{2,0,1:T(4,128)S(1)}, f32[4,64,256]{2,0,1:T(4,128)}, u32[]{:S(2)}, u32[]{:S(2)}) collective-permute-start(f32[4,64,256]{2,0,1:T(4,128)S(1)} %collective-permute-done.32), channel_id=1, source_target_pairs={{0,96},{32,0},{64,32},{96,64},{128,224},{160,128},{192,160},{224,1... | collective-permute-start | bytes 786440 | tf_op jit(solution)/shard_map/ppermute | solution.py:67
  258.6 20.3 %collective-permute-start.27 = (f32[4,64,256]{2,0,1:T(4,128)}, f32[4,64,256]{2,0,1:T(4,128)S(1)}, u32[]{:S(2)}, u32[]{:S(2)}) collective-permute-start(f32[4,64,256]{2,0,1:T(4,128)} %collective-permute-done.25), channel_id=1, source_target_pairs={{0,96},{32,0},{64,32},{96,64},{128,224},{160,128},{192,160},{224,1... | collective-permute-start | bytes 786440 | tf_op jit(solution)/shard_map/ppermute | solution.py:67
